TPU v7x, 256 devices: a whole 4x4x8 slice. The times are simulated.
256 devices in a mesh: pix: 32 (over z, x), feat: 8 (over y, core).
Axes of the slice: x: 4, y: 4, z: 8, core: 2. Of those that a mesh axis runs over, the one named last changes fastest.
Arguments:
- mass_bin: int32 [262144, 256], P(('pix', 'feat')), may hold values from 0 to 255
- mobility_bin: int32 [262144, 256], P(('pix', 'feat')), may hold values from 0 to 15
- intensity: bfloat16 [262144, 256], P(('pix', 'feat')), may hold values from 10 to 4000, as said below
- basis_init: float32 [262144, 64], P(('pix', 'feat')), may hold values from 0.1 to 1
- profile_init: float32 [64, 4096], P(None, 'feat'), may hold values from 0.1 to 1
Outputs:
- basis: float32 [262144, 64], P(('pix', 'feat'))
- profiles: float32 [64, 4096], P(None, 'feat')
Inputs may be any that keep to these rules, and one draw needn't show every extreme that they name: `intensity`: positive peak intensities.
All inputs are finite; a program needn't handle non-finite values.
Results may differ from a plain program's by a relative error of at most 0.00045.
Values may be sent and summed in bfloat16 or wider, within the bound.
No kernel may reach another device: no remote copies, remote signals or barrier semaphores. Data moves between devices by JAX's collectives and lax.ppermute only.
A program may use at most 64 MiB of HBM per device.

v0:
```python
import math
import jax
import jax.numpy as jnp
from jax import lax
from jax.sharding import PartitionSpec as P

MZ = 256
MOB = 16
PEAKS = 256
ITERS = 2
EPS = 1e-06


def bin_block(args):
    mass, mobility, weight = args
    mass_hot = (mass[:, :, None] == jnp.arange(MZ, dtype=jnp.int32)[None, None, :]).astype(
        jnp.bfloat16
    ) * weight[:, :, None]
    mobility_hot = (mobility[:, :, None] == jnp.arange(MOB, dtype=jnp.int32)[None, None, :]).astype(
        jnp.bfloat16
    )
    dense = jnp.einsum("pkb,pkm->pbm", mobility_hot, mass_hot, preferred_element_type=jnp.float32)
    return dense.reshape(mass.shape[0], MZ * MOB).astype(jnp.bfloat16)


def local(mass_bin, mobility_bin, intensity, basis_init, profile_init):
    rows = mass_bin.shape[0]
    block = math.gcd(rows, 32)
    count = rows // block
    spectra = lax.map(
        bin_block,
        (
            mass_bin.reshape(count, block, PEAKS),
            mobility_bin.reshape(count, block, PEAKS),
            intensity.reshape(count, block, PEAKS),
        ),
    )
    spectra = spectra.reshape(rows, MZ * MOB)
    highest = lax.Precision.HIGHEST
    basis, profiles = (basis_init, profile_init)
    for step in range(ITERS):
        partial_h = lax.dot_general(
            basis.astype(jnp.bfloat16),
            spectra,
            (((0,), (0,)), ((), ())),
            preferred_element_type=jnp.float32,
        )
        partial_gram = lax.dot_general(
            basis,
            basis,
            (((0,), (0,)), ((), ())),
            precision=highest,
            preferred_element_type=jnp.float32,
        )
        shared = lax.psum_scatter(partial_h, "feat", scatter_dimension=1, tiled=True)
        numer_h = lax.psum(shared, "pix")
        gram_w = lax.psum(partial_gram, ("pix", "feat"))
        profiles = (
            profiles
            * numer_h
            / (
                jnp.dot(gram_w, profiles, precision=highest, preferred_element_type=jnp.float32)
                + EPS
            )
        )
        numer_w = lax.dot_general(
            spectra,
            lax.all_gather(profiles.astype(jnp.bfloat16), "feat", axis=1, tiled=True),
            (((1,), (1,)), ((), ())),
            preferred_element_type=jnp.float32,
        )
        local_gram = lax.dot_general(
            profiles,
            profiles,
            (((1,), (1,)), ((), ())),
            precision=highest,
            preferred_element_type=jnp.float32,
        )
        gram_h = lax.psum(local_gram, "feat")
        basis = (
            basis
            * numer_w
            / (jnp.dot(basis, gram_h, precision=highest, preferred_element_type=jnp.float32) + EPS)
        )
    return (basis, profiles)


def solution(mesh):
    return jax.shard_map(
        local,
        mesh=mesh,
        in_specs=(
            P(("pix", "feat"), None),
            P(("pix", "feat"), None),
            P(("pix", "feat"), None),
            P(("pix", "feat"), None),
            P(None, "feat"),
        ),
        out_specs=(P(("pix", "feat"), None), P(None, "feat")),
        check_vma=False,
    )
```

profile of v0, /device:TPU:2, one launch (start us, length us, event | category | flops | bytes accessed | tf_op | source)
XLA Modules:
  0.0 668.2 jit_solution(15157433333801755827)
XLA Ops:
  7.2 192.9 %while.10 = (s32[]{:T(128)}, bf16[32,32,4096]{2,1,0:T(8,128)(2,1)}, s32[32,32,256]{2,1,0:T(8,128)}, s32[32,32,256]{2,1,0:T(8,128)}, bf16[32,32,256]{2,1,0:T(8,128)(2,1)}, /*index=5*/s32[]{:T(128)}) while((s32[]{:T(128)}, bf16[32,32,4096]{2,1,0:T(8,128)(2,1)}, s32[32,32,256]{2,1,0:T(8,128)}, s32[32,32,256]{2,1,0:T(8,128)}, ...), condition=%wide.region_1.2_spmd, body=%wide.region_0.1_spmd.sunk | while | flops 71565312 | bytes 1557069 | solution.py:30
  8.8 3.7 fusion.50
  14.8 3.7 fusion.50
  20.8 3.7 fusion.50
  26.8 3.7 fusion.50
  32.9 3.7 fusion.50
  38.9 3.7 fusion.50
  44.9 3.7 fusion.50
  51.0 3.7 fusion.50
  105.2 3.7 fusion.50
  200.1 6.1 convolution_bitcast_fusion
  206.2 37.5 %reduce-scatter.3.cloned.1.call-done = f32[64,512]{1,0:T(8,128)} async-done(((f32[64,4096]{1,0:T(8,128)}), f32[64,512]{1,0:T(8,128)}) %reduce-scatter.3.cloned.1.call-update) | async-done | bytes 131088 | tf_op jit(solution)/shard_map/reduce_scatter | solution.py:55
  244.2 74.5 %psum.43 = f32[64,64]{1,0:T(8,128)S(1)} all-reduce(f32[64,64]{1,0:T(8,128)S(1)} %fusion.21), channel_id=1, replica_groups=mesh['pix'=32,'feat'=8] {'pix','feat'}, use_global_device_ids=true, to_apply=%region_4.5 | all-reduce | flops 4096 | bytes 32768 | tf_op jit(solution)/shard_map/psum | solution.py:57
  318.7 68.1 %all-reduce.3.cloned.1.call-done = f32[64,512]{1,0:T(8,128)} async-done(((f32[64,512]{1,0:T(8,128)}), f32[64,512]{1,0:T(8,128)}) %all-reduce.3.cloned.1.call-update) | async-done | bytes 131088 | tf_op jit(solution)/shard_map/psum | solution.py:56
  388.0 13.5 %all_gather.6 = bf16[64,4096]{1,0:T(8,128)(2,1)S(1)} all-gather(bf16[64,512]{1,0:T(8,128)(2,1)S(1)} %get-tuple-element.42), channel_id=1, replica_groups=mesh['pix'=32,'feat'=8] {'feat'}, dimensions={1}, use_global_device_ids=true | all-gather | bytes 589824 | tf_op jit(solution)/shard_map/all_gather | solution.py:68
  401.5 6.0 convolution_multiply_fusion.1
  407.8 25.8 %psum.44 = f32[64,64]{1,0:T(8,128)S(1)} all-reduce(f32[64,64]{1,0:T(8,128)S(1)} %fusion.22), channel_id=1, replica_groups=mesh['pix'=32,'feat'=8] {'feat'}, use_global_device_ids=true, to_apply=%region_5.6 | all-reduce | flops 4096 | bytes 32768 | tf_op jit(solution)/shard_map/psum | solution.py:79
  434.0 6.0 fusion.16
  440.1 30.4 %reduce-scatter.5.cloned.1.call-done = f32[64,512]{1,0:T(8,128)} async-done(((f32[64,4096]{1,0:T(8,128)}), f32[64,512]{1,0:T(8,128)}) %reduce-scatter.5.cloned.1.call-update) | async-done | bytes 131088 | tf_op jit(solution)/shard_map/reduce_scatter | solution.py:55
  470.8 74.4 %psum.46 = f32[64,64]{1,0:T(8,128)S(1)} all-reduce(f32[64,64]{1,0:T(8,128)S(1)} %fusion.23), channel_id=1, replica_groups=mesh['pix'=32,'feat'=8] {'pix','feat'}, use_global_device_ids=true, to_apply=%region_8.9 | all-reduce | flops 4096 | bytes 32768 | tf_op jit(solution)/shard_map/psum | solution.py:57
  545.2 68.6 %all-reduce.5.cloned.1.call-done = f32[64,512]{1,0:T(8,128)} async-done(((f32[64,512]{1,0:T(8,128)}), f32[64,512]{1,0:T(8,128)}) %all-reduce.5.cloned.1.call-update) | async-done | bytes 131088 | tf_op jit(solution)/shard_map/psum | solution.py:56
  615.0 13.4 %all_gather.7 = bf16[64,4096]{1,0:T(8,128)(2,1)S(1)} all-gather(bf16[64,512]{1,0:T(8,128)(2,1)S(1)} %get-tuple-element.44), channel_id=1, replica_groups=mesh['pix'=32,'feat'=8] {'feat'}, dimensions={1}, use_global_device_ids=true | all-gather | bytes 589824 | tf_op jit(solution)/shard_map/all_gather | solution.py:68
  628.5 6.0 convolution_multiply_fusion
  634.8 25.8 %psum.47 = f32[64,64]{1,0:T(8,128)S(1)} all-reduce(f32[64,64]{1,0:T(8,128)S(1)} %fusion.24), channel_id=1, replica_groups=mesh['pix'=32,'feat'=8] {'feat'}, use_global_device_ids=true, to_apply=%region_9.10 | all-reduce | flops 4096 | bytes 32768 | tf_op jit(solution)/shard_map/psum | solution.py:79
  (174 shorter events, 165.0 us)
Async XLA Ops:
  7.2 236.6 %reduce-scatter.3.cloned.1.call-start = ((), (), s32[]{:S(2)}) async-start(), calls=%async_computation.2 | async-start | bytes 1179648 | tf_op jit(solution)/shard_map/reduce_scatter | solution.py:55
  7.2 192.9 %copy-start = (f32[1024,64]{0,1:T(8,128)S(1)}, f32[1024,64]{0,1:T(8,128)}, u32[]{:S(2)}) copy-start(f32[1024,64]{0,1:T(8,128)} %param.10) | copy-start | bytes 786436
  200.1 186.7 %copy-start.2 = (f32[64,512]{1,0:T(8,128)S(1)}, f32[64,512]{1,0:T(8,128)}, u32[]{:S(2)}) copy-start(f32[64,512]{1,0:T(8,128)} %param.11) | copy-start | bytes 393220
  206.2 180.6 %all-reduce.3.cloned.1.call-start = ((), (), s32[]{:S(2)}) async-start(), calls=%async_computation.3 | async-start | bytes 262144 | tf_op jit(solution)/shard_map/psum | solution.py:56
  243.8 226.7 %reduce-scatter.5.cloned.1.call-start = ((), (), s32[]{:S(2)}) async-start(), calls=%async_computation.4 | async-start | bytes 1179648 | tf_op jit(solution)/shard_map/reduce_scatter | solution.py:55
  440.0 173.8 %all-reduce.5.cloned.1.call-start = ((), (), s32[]{:S(2)}) async-start(), calls=%async_computation.5 | async-start | bytes 262144 | tf_op jit(solution)/shard_map/psum | solution.py:56
  615.0 46.7 %copy-start.1 = (f32[64,512]{1,0:T(8,128)}, f32[64,512]{1,0:T(8,128)S(1)}, u32[]{:S(2)}) copy-start(f32[64,512]{1,0:T(8,128)S(1)} %get-tuple-element.45) | copy-start | bytes 393220
Sparse Core Ops, SparseCore 0:
  206.3 37.3 reduce-scatter.2
  247.2 139.5 all-reduce.2
  440.1 30.2 reduce-scatter.4
  474.1 139.6 all-reduce.4
where the time goes:
time: 673 us; the launch traced here: 668 us
  blocking collectives  227 us (34%)
  waiting for transfers between devices  205 us (30%)
  matrix products  146 us (22%)
  local copies, waits for them, and re-layouts  75.5 us (11%)
  between operations  13.8 us (2%)
    psum x2, blocking collectives, local(): gram_w = lax.psum(partial_gram, ('pix', 'feat'))  149 us
    psum x2, waiting for transfers between devices, local(): numer_h = lax.psum(shared, 'pix')  137 us
    dot_general x32, matrix products, bin_block(): jnp.einsum('pkb,pkm->pbm', mobility_hot, mass_hot, preferred_element_type...  117 us
    reduce_scatter x2, waiting for transfers between devices, local(): lax.psum_scatter(partial_h, 'feat', scatter_dimension=1, tiled=True)  67.8 us
    psum x2, blocking collectives, local(): gram_h = lax.psum(local_gram, 'feat')  51.6 us
    all_gather x2, blocking collectives, local(): lax.all_gather(profiles.astype(jnp.bfloat16), 'feat', axis=1, tiled=True)  26.9 us
    eq x32, local copies, waits for them, and re-layouts, bin_block(): mass[:, :, None] == jnp.arange(MZ, dtype=jnp.int32)[None, None, :]  25 us
    dynamic_update_slice x32, local copies, waits for them, and re-layouts, local(): lax.map(bin_block, (mass_bin.reshape(count, block, PEAKS), mobility_bin.r...  23.4 us
  transfers between devices with their start and end apart: 4, of which 4 were waited for; matrix products, arithmetic and copies ran while one was open for 0% of the time, Pallas kernels for 0%

commit v1 on v0

--- a/solution.py
+++ b/solution.py
@@ -54,7 +54,9 @@
         )
         shared = lax.psum_scatter(partial_h, "feat", scatter_dimension=1, tiled=True)
         numer_h = lax.psum(shared, "pix")
-        gram_w = lax.psum(partial_gram, ("pix", "feat"))
+        gram_w = partial_gram
+        for axis in ("pix", "feat"):
+            gram_w = lax.psum(gram_w, axis)
         profiles = (
             profiles
             * numer_h

time: 673 us -> 712 us (1.058)
  blocking collectives: 227 us -> 397 us
  waiting for transfers between devices: 205 us -> 70.8 us
    psum x2 -> x4, blocking collectives: 149 us -> 324 us  [local(): gram_w = lax.psum(gram_w, axis)]
    psum x2, waiting for transfers between devices: 137 us -> 0.01 us  [local(): numer_h = lax.psum(shared, 'pix')]
  transfers between devices with their start and end apart: 4 -> 4, of which waited for: 4 -> 2; matrix products, arithmetic and copies ran while one was open for 0% -> 0% of each run, Pallas kernels for 0% -> 0%
where the time goes in v1:
time: 712 us; the launch traced here: 704 us
  blocking collectives  397 us (56%)
  matrix products  146 us (21%)
  local copies, waits for them, and re-layouts  75.5 us (11%)
  waiting for transfers between devices  70.8 us (10%)
  between operations  13.8 us (2%)
    psum x4, blocking collectives, local(): gram_w = lax.psum(gram_w, axis)  324 us
    dot_general x32, matrix products, bin_block(): jnp.einsum('pkb,pkm->pbm', mobility_hot, mass_hot, preferred_element_type...  117 us
    reduce_scatter x2, waiting for transfers between devices, local(): lax.psum_scatter(partial_h, 'feat', scatter_dimension=1, tiled=True)  70.8 us
    psum x2, blocking collectives, local(): gram_h = lax.psum(local_gram, 'feat')  47.6 us
    all_gather x2, blocking collectives, local(): lax.all_gather(profiles.astype(jnp.bfloat16), 'feat', axis=1, tiled=True)  26.2 us
    eq x32, local copies, waits for them, and re-layouts, bin_block(): mass[:, :, None] == jnp.arange(MZ, dtype=jnp.int32)[None, None, :]  25 us
    dynamic_update_slice x32, local copies, waits for them, and re-layouts, local(): lax.map(bin_block, (mass_bin.reshape(count, block, PEAKS), mobility_bin.r...  23.4 us
    mul x32, local copies, waits for them, and re-layouts, bin_block(): (mass[:, :, None] == jnp.arange(MZ, dtype=jnp.int32)[None, None, :]).asty...  23 us
  transfers between devices with their start and end apart: 4, of which 2 were waited for; matrix products, arithmetic and copies ran while one was open for 0% of the time, Pallas kernels for 0%

profile of v1, /device:TPU:2, one launch (start us, length us, event | category | flops | bytes accessed | tf_op | source)
XLA Modules:
  0.0 704.4 jit_solution(3100505389470967569)
XLA Ops:
  7.2 192.9 %while.10 = (s32[]{:T(128)}, bf16[32,32,4096]{2,1,0:T(8,128)(2,1)}, s32[32,32,256]{2,1,0:T(8,128)}, s32[32,32,256]{2,1,0:T(8,128)}, bf16[32,32,256]{2,1,0:T(8,128)(2,1)}, /*index=5*/s32[]{:T(128)}) while((s32[]{:T(128)}, bf16[32,32,4096]{2,1,0:T(8,128)(2,1)}, s32[32,32,256]{2,1,0:T(8,128)}, s32[32,32,256]{2,1,0:T(8,128)}, ...), condition=%wide.region_1.2_spmd, body=%wide.region_0.1_spmd.sunk | while | flops 71565312 | bytes 1557069 | solution.py:30
  8.8 3.7 fusion.50
  14.8 3.7 fusion.50
  20.8 3.7 fusion.50
  26.8 3.7 fusion.50
  32.9 3.7 fusion.50
  38.9 3.7 fusion.50
  44.9 3.7 fusion.50
  51.0 3.7 fusion.50
  105.2 3.7 fusion.50
  200.1 6.1 convolution_bitcast_fusion
  206.2 37.5 %reduce-scatter.3.cloned.1.call-done = f32[64,512]{1,0:T(8,128)} async-done(((f32[64,4096]{1,0:T(8,128)}), f32[64,512]{1,0:T(8,128)}) %reduce-scatter.3.cloned.1.call-update) | async-done | bytes 131088 | tf_op jit(solution)/shard_map/reduce_scatter | solution.py:55
  244.2 138.1 %psum.57 = f32[64,64]{1,0:T(8,128)S(1)} all-reduce(f32[64,64]{1,0:T(8,128)S(1)} %fusion.21), channel_id=1, replica_groups=mesh['pix'=32,'feat'=8] {'pix'}, use_global_device_ids=true, to_apply=%region_4.5 | all-reduce | flops 4096 | bytes 32768 | tf_op jit(solution)/shard_map/psum | solution.py:59
  382.2 23.6 %psum.58 = f32[64,64]{1,0:T(8,128)S(1)} all-reduce(f32[64,64]{1,0:T(8,128)S(1)} %psum.57), channel_id=1, replica_groups=mesh['pix'=32,'feat'=8] {'feat'}, use_global_device_ids=true, to_apply=%region_5.6 | all-reduce | flops 4096 | bytes 32768 | tf_op jit(solution)/shard_map/psum | solution.py:59
  407.0 13.1 %all_gather.6 = bf16[64,4096]{1,0:T(8,128)(2,1)S(1)} all-gather(bf16[64,512]{1,0:T(8,128)(2,1)S(1)} %get-tuple-element.42), channel_id=1, replica_groups=mesh['pix'=32,'feat'=8] {'feat'}, dimensions={1}, use_global_device_ids=true | all-gather | bytes 589824 | tf_op jit(solution)/shard_map/all_gather | solution.py:70
  420.1 6.0 convolution_multiply_fusion.1
  426.4 23.8 %psum.59 = f32[64,64]{1,0:T(8,128)S(1)} all-reduce(f32[64,64]{1,0:T(8,128)S(1)} %fusion.22), channel_id=1, replica_groups=mesh['pix'=32,'feat'=8] {'feat'}, use_global_device_ids=true, to_apply=%region_6.7 | all-reduce | flops 4096 | bytes 32768 | tf_op jit(solution)/shard_map/psum | solution.py:81
  450.6 6.0 fusion.16
  456.7 33.3 %reduce-scatter.5.cloned.1.call-done = f32[64,512]{1,0:T(8,128)} async-done(((f32[64,4096]{1,0:T(8,128)}), f32[64,512]{1,0:T(8,128)}) %reduce-scatter.5.cloned.1.call-update) | async-done | bytes 131088 | tf_op jit(solution)/shard_map/reduce_scatter | solution.py:55
  490.4 138.1 %psum.61 = f32[64,64]{1,0:T(8,128)S(1)} all-reduce(f32[64,64]{1,0:T(8,128)S(1)} %fusion.23), channel_id=1, replica_groups=mesh['pix'=32,'feat'=8] {'pix'}, use_global_device_ids=true, to_apply=%region_9.10 | all-reduce | flops 4096 | bytes 32768 | tf_op jit(solution)/shard_map/psum | solution.py:59
  628.5 23.8 %psum.62 = f32[64,64]{1,0:T(8,128)S(1)} all-reduce(f32[64,64]{1,0:T(8,128)S(1)} %psum.61), channel_id=1, replica_groups=mesh['pix'=32,'feat'=8] {'feat'}, use_global_device_ids=true, to_apply=%region_10.11 | all-reduce | flops 4096 | bytes 32768 | tf_op jit(solution)/shard_map/psum | solution.py:59
  653.5 13.1 %all_gather.7 = bf16[64,4096]{1,0:T(8,128)(2,1)S(1)} all-gather(bf16[64,512]{1,0:T(8,128)(2,1)S(1)} %get-tuple-element.44), channel_id=1, replica_groups=mesh['pix'=32,'feat'=8] {'feat'}, dimensions={1}, use_global_device_ids=true | all-gather | bytes 589824 | tf_op jit(solution)/shard_map/all_gather | solution.py:70
  666.6 6.0 convolution_multiply_fusion
  672.9 23.8 %psum.63 = f32[64,64]{1,0:T(8,128)S(1)} all-reduce(f32[64,64]{1,0:T(8,128)S(1)} %fusion.24), channel_id=1, replica_groups=mesh['pix'=32,'feat'=8] {'feat'}, use_global_device_ids=true, to_apply=%region_11.12 | all-reduce | flops 4096 | bytes 32768 | tf_op jit(solution)/shard_map/psum | solution.py:81
  (176 shorter events, 165.0 us)
Async XLA Ops:
  7.2 236.6 %reduce-scatter.3.cloned.1.call-start = ((), (), s32[]{:S(2)}) async-start(), calls=%async_computation.2 | async-start | bytes 1179648 | tf_op jit(solution)/shard_map/reduce_scatter | solution.py:55
  7.2 192.9 %copy-start = (f32[1024,64]{0,1:T(8,128)S(1)}, f32[1024,64]{0,1:T(8,128)}, u32[]{:S(2)}) copy-start(f32[1024,64]{0,1:T(8,128)} %param.10) | copy-start | bytes 786436
  200.1 205.7 %copy-start.2 = (f32[64,512]{1,0:T(8,128)S(1)}, f32[64,512]{1,0:T(8,128)}, u32[]{:S(2)}) copy-start(f32[64,512]{1,0:T(8,128)} %param.11) | copy-start | bytes 393220
  206.2 199.6 %all-reduce.3.cloned.1.call-start = ((), (), s32[]{:S(2)}) async-start(), calls=%async_computation.3 | async-start | bytes 262144 | tf_op jit(solution)/shard_map/psum | solution.py:56
  243.8 246.3 %reduce-scatter.5.cloned.1.call-start = ((), (), s32[]{:S(2)}) async-start(), calls=%async_computation.4 | async-start | bytes 1179648 | tf_op jit(solution)/shard_map/reduce_scatter | solution.py:55
  456.7 195.6 %all-reduce.5.cloned.1.call-start = ((), (), s32[]{:S(2)}) async-start(), calls=%async_computation.5 | async-start | bytes 262144 | tf_op jit(solution)/shard_map/psum | solution.py:56
  653.5 44.3 %copy-start.1 = (f32[64,512]{1,0:T(8,128)}, f32[64,512]{1,0:T(8,128)S(1)}, u32[]{:S(2)}) copy-start(f32[64,512]{1,0:T(8,128)S(1)} %get-tuple-element.45) | copy-start | bytes 393220
Sparse Core Ops, SparseCore 0:
  206.3 37.3 reduce-scatter.2
  247.2 139.5 all-reduce.2
  456.8 33.1 reduce-scatter.4
  493.7 139.5 all-reduce.4
